TPU v7x, 256 devices: a whole 4x4x8 slice. The times are simulated.
256 devices in a mesh: grp: 32 (over x, z), shard: 8 (over y, core).
Axes of the slice: x: 4, y: 4, z: 8, core: 2. Of those that a mesh axis runs over, the one named last changes fastest.
Arguments:
- layer_inputs: bfloat16 [131072, 1600], P(('grp', 'shard')), may hold values from -6 to 6
- cotangents: bfloat16 [131072, 1600], P(('grp', 'shard')), may hold values from -0.25 to 0.25
- weight: bfloat16 [1600, 1600], P('shard'), may hold values from -0.15625 to 0.15625
- error_state: float32 [32, 1600, 1600], P('grp', 'shard'), may hold values from -6 to 6
- momentum: float32 [1600, 1600], P('shard'), may hold values from -0.75 to 0.75
- bias_momentum: float32 [1600], replicated, may hold values from -6 to 6
- start_basis: float32 [1600, 32], replicated, may hold values from -6 to 6
- next_inputs: bfloat16 [131072, 1600], P(('grp', 'shard')), may hold values from -6 to 6
Outputs:
- next_outputs: bfloat16 [131072, 1600], P(('grp', 'shard'))
- new_error: float32 [32, 1600, 1600], P('grp', 'shard')
- new_momentum: float32 [1600, 1600], P('shard')
- new_bias_momentum: float32 [1600], replicated
All inputs are finite; a program needn't handle non-finite values.
Results may differ from a plain program's by a relative error of at most 0.015.
Values may be sent and summed in bfloat16 or wider, within the bound.
No kernel may reach another device: no remote copies, remote signals or barrier semaphores. Data moves between devices by JAX's collectives and lax.ppermute only.
A program may use at most 128 MiB of HBM per device.

v0:
```python
import jax
import jax.numpy as jnp
from jax import lax
from jax.sharding import PartitionSpec as P

momentum_decay = 0.9
learn_rate = 0.1


def shards(
    layer_inputs, cotangents, weight, error_state, momentum, bias_momentum, start_basis, next_inputs
):
    highest = lax.Precision.HIGHEST
    group_count = lax.axis_size("grp")
    columns = layer_inputs
    gradient = lax.psum_scatter(
        lax.dot_general(
            columns, cotangents, (((0,), (0,)), ((), ())), preferred_element_type=jnp.float32
        ).astype(jnp.bfloat16),
        "shard",
        scatter_dimension=0,
        tiled=True,
    ).astype(jnp.float32)
    column_sums = lax.psum(jnp.sum(cotangents, axis=0, dtype=jnp.float32), ("grp", "shard"))
    corrected = gradient + error_state[0]
    basis = start_basis
    ortho = start_basis
    for round_index in range(2):
        local_factor = jnp.dot(corrected, basis, precision=highest)
        own_rows = lax.psum(local_factor, "grp")
        gram = lax.psum(jnp.dot(own_rows.T, own_rows, precision=highest), "shard")
        lower_factor = jnp.linalg.cholesky(gram)
        ortho = jax.scipy.linalg.solve_triangular(lower_factor, own_rows.T, lower=True).T
        partial_basis = lax.dot_general(
            corrected, ortho, (((0,), (0,)), ((), ())), precision=highest
        )
        summed = lax.psum(partial_basis, ("grp", "shard"))
        basis = summed / group_count
    approx = jnp.dot(ortho, basis.T, precision=highest)
    new_error = (corrected - approx)[None, :, :]
    new_momentum = momentum_decay * momentum + approx
    new_bias_momentum = momentum_decay * bias_momentum + column_sums / group_count
    new_weight = (weight.astype(jnp.float32) - learn_rate * new_momentum).astype(jnp.bfloat16)
    columns = next_inputs
    projected = jnp.dot(
        columns,
        lax.all_gather(new_weight, "shard", axis=0, tiled=True),
        preferred_element_type=jnp.float32,
    )
    return (projected.astype(jnp.bfloat16), new_error, new_momentum, new_bias_momentum)


def solution(mesh):
    placed = (
        P(("grp", "shard"), None),
        P(("grp", "shard"), None),
        P("shard", None),
        P("grp", "shard", None),
        P("shard", None),
        P(),
        P(),
        P(("grp", "shard"), None),
    )
    return jax.shard_map(
        shards,
        mesh=mesh,
        in_specs=placed,
        out_specs=(P(("grp", "shard"), None), P("grp", "shard", None), P("shard", None), P()),
        check_vma=False,
    )
```

profile of v0, /device:TPU:1, one launch (start us, length us, event | category | flops | bytes accessed | tf_op | source)
XLA Modules:
  0.0 1017.4 jit_solution(5363052511592432300)
XLA Ops:
  7.2 0.0 copy-start
  7.2 0.0 reduce-scatter.4.cloned.1.call-start
  7.2 1.4 copy-done
  8.6 6.3 convolution_convert_fusion
  14.9 0.0 copy-start.1
  14.9 0.0 copy-start.2
  14.9 0.0 reduce-scatter.4.cloned.1.call-update
  15.0 0.0 all-reduce.4.cloned.1.call-start
  15.0 50.3 %reduce-scatter.4.cloned.1.call-done = bf16[200,1600]{1,0:T(8,128)(2,1)} async-done(((bf16[1600,1600]{1,0:T(8,128)(2,1)}), bf16[200,1600]{1,0:T(8,128)(2,1)}) %reduce-scatter.4.cloned.1.call-update) | async-done | bytes 640016
  65.3 0.0 copy-done.1
  65.3 0.0 copy-done.2
  65.3 2.4 fusion.23
  67.8 115.4 %psum.49 = f32[200,32]{0,1:T(8,128)S(1)} all-reduce(f32[200,32]{0,1:T(8,128)S(1)} %fusion.23), channel_id=1, replica_groups=mesh['grp'=32,'shard'=8] {'grp'}, use_global_device_ids=true, to_apply=%region_1.0 | all-reduce | flops 6400 | bytes 51200 | tf_op jit(solution)/shard_map/psum | solution.py:30
  183.2 0.2 fusion.26
  183.4 51.6 %psum.50 = f32[32,32]{0,1:T(8,128)S(1)} all-reduce(f32[32,32]{0,1:T(8,128)S(1)} %fusion.26), channel_id=1, replica_groups=mesh['grp'=32,'shard'=8] {'shard'}, use_global_device_ids=true, to_apply=%region_2.0 | all-reduce | flops 1024 | bytes 8192 | tf_op jit(solution)/shard_map/psum | solution.py:31
  234.9 0.1 copy.17
  235.0 2.9 cholesky.44
  238.0 0.6 compare_reduce_fusion.1
  238.6 0.7 fusion.11
  239.3 2.4 custom-call.6
  241.7 0.2 fusion.9
  242.0 4.8 fusion.22
  246.7 0.0 all-reduce.4.cloned.1.call-update
  246.8 0.0 all-reduce.6.cloned.1.call-start
  246.8 248.4 %all-reduce.4.cloned.1.call-done = f32[1600,32]{1,0:T(8,128)} async-done(((f32[1600,32]{1,0:T(8,128)}), f32[1600,32]{1,0:T(8,128)}) %all-reduce.4.cloned.1.call-update) | async-done | bytes 204816 | tf_op jit(solution)/shard_map/psum | solution.py:37
  495.2 2.9 fusion.3
  498.1 114.1 %psum.52 = f32[200,32]{0,1:T(8,128)S(1)} all-reduce(f32[200,32]{0,1:T(8,128)S(1)} %fusion.3), channel_id=1, replica_groups=mesh['grp'=32,'shard'=8] {'grp'}, use_global_device_ids=true, to_apply=%region_6.0 | all-reduce | flops 6400 | bytes 51200 | tf_op jit(solution)/shard_map/psum | solution.py:30
  612.2 0.2 fusion.27
  612.4 46.1 %psum.53 = f32[32,32]{0,1:T(8,128)S(1)} all-reduce(f32[32,32]{0,1:T(8,128)S(1)} %fusion.27), channel_id=1, replica_groups=mesh['grp'=32,'shard'=8] {'shard'}, use_global_device_ids=true, to_apply=%region_7.0 | all-reduce | flops 1024 | bytes 8192 | tf_op jit(solution)/shard_map/psum | solution.py:31
  658.5 0.1 copy.19
  658.6 2.9 cholesky.55
  661.6 0.6 compare_reduce_fusion
  662.2 0.7 fusion.12
  662.9 2.4 custom-call.7
  665.3 0.2 fusion.7
  665.5 4.8 fusion.21
  670.3 0.0 all-reduce.6.cloned.1.call-update
  670.4 0.0 all-gather.2.cloned.1.call-start
  670.4 248.4 %all-reduce.6.cloned.1.call-done = f32[1600,32]{1,0:T(8,128)} async-done(((f32[1600,32]{1,0:T(8,128)}), f32[1600,32]{1,0:T(8,128)}) %all-reduce.6.cloned.1.call-update) | async-done | bytes 204816 | tf_op jit(solution)/shard_map/psum | solution.py:37
  918.8 5.3 subtract_convert_fusion
  924.0 0.0 copy-start.3
  924.1 0.0 all-gather.2.cloned.1.call-update
  924.1 1.7 convert_reduce_fusion
  925.8 77.1 %psum.55 = f32[1600]{0:T(1024)S(1)} all-reduce(f32[1600]{0:T(1024)S(1)} %convert_reduce_fusion), channel_id=1, replica_groups=mesh['grp'=32,'shard'=8] {'grp','shard'}, use_global_device_ids=true, to_apply=%region_10.13 | all-reduce | flops 1600 | bytes 12800 | tf_op jit(solution)/shard_map/psum | solution.py:24
  1002.9 0.0 copy-done.3
  1002.9 0.6 multiply_add_fusion.1
  1003.5 0.0 all-gather.2.cloned.1.call-done
  1003.5 7.4 fusion
  (4 shorter events, 0.1 us)
Async XLA Ops:
  7.2 1.4 copy-start
  7.2 58.1 %reduce-scatter.4.cloned.1.call-start = ((), (), s32[]{:S(2)}) async-start(), calls=%async_computation.4 | async-start | bytes 5990400
  14.9 50.4 %copy-start.1 = (f32[1,200,1600]{2,1,0:T(8,128)S(1)}, f32[1,200,1600]{2,1,0:T(8,128)}, u32[]{:S(2)}) copy-start(f32[1,200,1600]{2,1,0:T(8,128)} %param.14) | copy-start | bytes 3840004
  14.9 50.4 %copy-start.2 = (f32[1600,32]{0,1:T(8,128)S(1)}, f32[1600,32]{0,1:T(8,128)}, u32[]{:S(2)}) copy-start(f32[1600,32]{0,1:T(8,128)} %param.17) | copy-start | bytes 614404
  15.0 480.3 %all-reduce.4.cloned.1.call-start = ((), (), s32[]{:S(2)}) async-start(), calls=%async_computation.1 | async-start | bytes 1638400 | tf_op jit(solution)/shard_map/psum | solution.py:37
  246.8 672.0 %all-reduce.6.cloned.1.call-start = ((), (), s32[]{:S(2)}) async-start(), calls=%async_computation.2 | async-start | bytes 1638400 | tf_op jit(solution)/shard_map/psum | solution.py:37
  670.4 333.1 %all-gather.2.cloned.1.call-start = ((), (), s32[]{:S(2)}) async-start(), calls=%async_computation.3 | async-start | bytes 5990400 | tf_op jit(solution)/shard_map/all_gather | solution.py:47
  924.0 78.8 %copy-start.3 = (f32[1600]{0:T(1024)S(1)}, f32[1600]{0:T(1024)}, u32[]{:S(2)}) copy-start(f32[1600]{0:T(1024)} %param.16) | copy-start | bytes 19204
Sparse Core Ops, SparseCore 0:
  15.1 50.1 reduce-scatter.3
  246.9 248.2 all-reduce.3
  670.5 248.2 all-reduce.5
  924.2 38.9 all-gather.1
where the time goes:
time: 1020 us
  waiting for transfers between devices  547 us (54%)
  blocking collectives  404 us (40%)
  matrix products  34.6 us (3%)
  other arithmetic  15.7 us (2%)
  between operations  13.8 us (1%)
    psum x2, waiting for transfers between devices, shards(): summed = lax.psum(partial_basis, ('grp', 'shard'))  497 us
    psum x2, blocking collectives, shards(): own_rows = lax.psum(local_factor, 'grp')  230 us
    psum x2, blocking collectives, shards(): gram = lax.psum(jnp.dot(own_rows.T, own_rows, precision=highest), 'shard')  97.7 us
    psum x1, blocking collectives, shards(): lax.psum(jnp.sum(cotangents, axis=0, dtype=jnp.float32), ('grp', 'shard'))  77.1 us
    unnamed x5, waiting for transfers between devices  50.4 us
  transfers between devices with their start and end apart: 4, of which 3 were waited for; matrix products, arithmetic and copies ran while one was open for 0% of the time, Pallas kernels for 0%

commit v1 on v0

--- a/solution.py
+++ b/solution.py
@@ -27,7 +27,11 @@
     ortho = start_basis
     for round_index in range(2):
         local_factor = jnp.dot(corrected, basis, precision=highest)
-        own_rows = lax.psum(local_factor, "grp")
+        own_rows = local_factor
+        for hop in (1, 2, 4, 8, 16):
+            own_rows = own_rows + lax.ppermute(
+                own_rows, "grp", [(dev, dev ^ hop) for dev in range(32)]
+            )
         gram = lax.psum(jnp.dot(own_rows.T, own_rows, precision=highest), "shard")
         lower_factor = jnp.linalg.cholesky(gram)
         ortho = jax.scipy.linalg.solve_triangular(lower_factor, own_rows.T, lower=True).T

time: 1020 us -> 802 us (0.79)
  blocking collectives: 404 us -> 134 us
  waiting for transfers between devices: 547 us -> 581 us
  starting transfers between devices: 0.16 us -> 21.7 us
    psum x2 -> x0, blocking collectives: 230 us -> none  [shards(): own_rows = lax.psum(local_factor, 'grp')]
    psum x2, blocking collectives: 97.7 us -> 56.3 us  [shards(): gram = lax.psum(jnp.dot(own_rows.T, own_rows, precision=highest), 'shard')]
    ppermute x0 -> x10, starting transfers between devices: none -> 21.5 us  [shards(): lax.ppermute(own_rows, 'grp', [(dev, dev ^ hop) for dev in range(32)])]
    ppermute x0 -> x10, waiting for transfers between devices: none -> 19.9 us  [shards(): lax.ppermute(own_rows, 'grp', [(dev, dev ^ hop) for dev in range(32)])]
    psum x2, waiting for transfers between devices: 497 us -> 511 us  [shards(): summed = lax.psum(partial_basis, ('grp', 'shard'))]
  transfers between devices with their start and end apart: 4 -> 14, of which waited for: 3 -> 13; matrix products, arithmetic and copies ran while one was open for 0% -> 0% of each run, Pallas kernels for 0% -> 0%
where the time goes in v1:
time: 802 us
  waiting for transfers between devices  581 us (72%)
  blocking collectives  134 us (17%)
  matrix products  34.6 us (4%)
  starting transfers between devices  21.7 us (3%)
  other arithmetic  15.8 us (2%)
  between operations  13.9 us (2%)
    psum x2, waiting for transfers between devices, shards(): summed = lax.psum(partial_basis, ('grp', 'shard'))  511 us
    psum x1, blocking collectives, shards(): lax.psum(jnp.sum(cotangents, axis=0, dtype=jnp.float32), ('grp', 'shard'))  77.2 us
    psum x2, blocking collectives, shards(): gram = lax.psum(jnp.dot(own_rows.T, own_rows, precision=highest), 'shard')  56.3 us
    unnamed x5, waiting for transfers between devices  50.4 us
    ppermute x10, starting transfers between devices, shards(): lax.ppermute(own_rows, 'grp', [(dev, dev ^ hop) for dev in range(32)])  21.5 us
    ppermute x10, waiting for transfers between devices, shards(): lax.ppermute(own_rows, 'grp', [(dev, dev ^ hop) for dev in range(32)])  19.9 us
  transfers between devices with their start and end apart: 14, of which 13 were waited for; matrix products, arithmetic and copies ran while one was open for 0% of the time, Pallas kernels for 0%

profile of v1, /device:TPU:1, one launch (start us, length us, event | category | flops | bytes accessed | tf_op | source)
XLA Modules:
  0.0 801.8 jit_solution(9507931167870537223)
XLA Ops:
  7.2 0.0 copy-start
  7.2 0.0 reduce-scatter.4.cloned.1.call-start
  7.2 1.4 copy-done
  8.6 6.3 convolution_convert_fusion
  14.9 0.0 copy-start.1
  14.9 0.0 copy-start.2
  14.9 0.0 reduce-scatter.4.cloned.1.call-update
  15.0 0.0 all-reduce.4.cloned.1.call-start
  15.0 50.3 %reduce-scatter.4.cloned.1.call-done = bf16[200,1600]{1,0:T(8,128)(2,1)} async-done(((bf16[1600,1600]{1,0:T(8,128)(2,1)}), bf16[200,1600]{1,0:T(8,128)(2,1)}) %reduce-scatter.4.cloned.1.call-update) | async-done | bytes 640016
  65.3 0.0 copy-done.1
  65.3 0.0 copy-done.2
  65.3 2.4 fusion.29
  67.8 1.5 collective-permute-start
  69.2 1.4 collective-permute-done
  70.6 2.4 collective-permute-start.1
  73.0 1.3 collective-permute-done.1
  74.3 5.9 collective-permute-start.2
  80.2 1.4 collective-permute-done.2
  81.6 1.1 collective-permute-start.3
  82.7 1.7 collective-permute-done.3
  84.4 2.7 collective-permute-start.4
  87.1 1.6 collective-permute-done.4
  88.6 0.2 fusion.23
  88.8 29.3 %psum.35 = f32[32,32]{0,1:T(8,128)S(1)} all-reduce(f32[32,32]{0,1:T(8,128)S(1)} %fusion.23), channel_id=1, replica_groups=mesh['grp'=32,'shard'=8] {'shard'}, use_global_device_ids=true, to_apply=%region_1.0 | all-reduce | flops 1024 | bytes 8192 | tf_op jit(solution)/shard_map/psum | solution.py:35
  118.1 0.1 copy.17
  118.2 2.9 cholesky.44
  121.1 0.6 compare_reduce_fusion.1
  121.8 0.7 fusion.11
  122.4 2.4 custom-call.6
  124.9 0.2 fusion.9
  125.1 4.8 fusion.28
  129.9 0.0 all-reduce.4.cloned.1.call-update
  129.9 0.0 all-reduce.6.cloned.1.call-start
  130.0 256.7 %all-reduce.4.cloned.1.call-done = f32[1600,32]{1,0:T(8,128)} async-done(((f32[1600,32]{1,0:T(8,128)}), f32[1600,32]{1,0:T(8,128)}) %all-reduce.4.cloned.1.call-update) | async-done | bytes 204816 | tf_op jit(solution)/shard_map/psum | solution.py:41
  386.7 2.9 fusion.3
  389.6 0.1 collective-permute-start.5
  389.7 2.8 collective-permute-done.5
  392.4 1.7 collective-permute-start.6
  394.2 1.9 collective-permute-done.6
  396.1 2.1 collective-permute-start.7
  398.2 4.6 collective-permute-done.7
  402.8 1.3 collective-permute-start.8
  404.1 1.8 collective-permute-done.8
  405.9 2.8 collective-permute-start.9
  408.6 1.5 collective-permute-done.9
  410.1 0.2 fusion.20
  410.3 27.0 %psum.37 = f32[32,32]{0,1:T(8,128)S(1)} all-reduce(f32[32,32]{0,1:T(8,128)S(1)} %fusion.20), channel_id=1, replica_groups=mesh['grp'=32,'shard'=8] {'shard'}, use_global_device_ids=true, to_apply=%region_5.0 | all-reduce | flops 1024 | bytes 8192 | tf_op jit(solution)/shard_map/psum | solution.py:35
  437.3 0.1 copy.19
  437.4 2.9 cholesky.55
  440.4 0.6 compare_reduce_fusion
  441.0 0.7 fusion.12
  441.7 2.4 custom-call.7
  444.1 0.2 fusion.7
  444.3 4.8 fusion.27
  449.1 0.0 all-reduce.6.cloned.1.call-update
  449.2 0.0 all-gather.2.cloned.1.call-start
  449.2 253.9 %all-reduce.6.cloned.1.call-done = f32[1600,32]{1,0:T(8,128)} async-done(((f32[1600,32]{1,0:T(8,128)}), f32[1600,32]{1,0:T(8,128)}) %all-reduce.6.cloned.1.call-update) | async-done | bytes 204816 | tf_op jit(solution)/shard_map/psum | solution.py:41
  703.1 5.3 subtract_convert_fusion
  708.4 0.0 all-gather.2.cloned.1.call-update
  708.4 1.7 convert_reduce_fusion
  710.1 77.2 %psum.39 = f32[1600]{0:T(1024)S(1)} all-reduce(f32[1600]{0:T(1024)S(1)} %convert_reduce_fusion), channel_id=1, replica_groups=mesh['grp'=32,'shard'=8] {'grp','shard'}, use_global_device_ids=true, to_apply=%region_8.11 | all-reduce | flops 1600 | bytes 12800 | tf_op jit(solution)/shard_map/psum | solution.py:24
  787.3 0.0 copy-done.3
  787.3 0.6 multiply_add_fusion.1
  787.9 7.4 fusion
  (14 shorter events, 0.1 us)
Async XLA Ops:
  7.2 1.4 copy-start
  7.2 58.1 %reduce-scatter.4.cloned.1.call-start = ((), (), s32[]{:S(2)}) async-start(), calls=%async_computation.4 | async-start | bytes 5990400
  14.9 50.4 %copy-start.1 = (f32[1,200,1600]{2,1,0:T(8,128)S(1)}, f32[1,200,1600]{2,1,0:T(8,128)}, u32[]{:S(2)}) copy-start(f32[1,200,1600]{2,1,0:T(8,128)} %param.14) | copy-start | bytes 3840004
  14.9 50.4 %copy-start.2 = (f32[1600,32]{0,1:T(8,128)S(1)}, f32[1600,32]{0,1:T(8,128)}, u32[]{:S(2)}) copy-start(f32[1600,32]{0,1:T(8,128)} %param.17) | copy-start | bytes 614404
  15.0 371.8 %all-reduce.4.cloned.1.call-start = ((), (), s32[]{:S(2)}) async-start(), calls=%async_computation.1 | async-start | bytes 1638400 | tf_op jit(solution)/shard_map/psum | solution.py:41
  67.8 2.9 collective-permute-start
  70.6 3.7 collective-permute-start.1
  74.3 7.3 collective-permute-start.2
  81.6 2.8 collective-permute-start.3
  84.4 4.3 collective-permute-start.4
  129.9 573.1 %all-reduce.6.cloned.1.call-start = ((), (), s32[]{:S(2)}) async-start(), calls=%async_computation.2 | async-start | bytes 1638400 | tf_op jit(solution)/shard_map/psum | solution.py:41
  389.6 2.9 collective-permute-start.5
  392.4 3.7 collective-permute-start.6
  396.1 6.7 collective-permute-start.7
  402.8 3.1 collective-permute-start.8
  405.9 4.3 collective-permute-start.9
  449.2 338.8 %all-gather.2.cloned.1.call-start = ((), (), s32[]{:S(2)}) async-start(), calls=%async_computation.3 | async-start | bytes 5990400 | tf_op jit(solution)/shard_map/all_gather | solution.py:51
  708.4 79.0 %copy-start.3 = (f32[1600]{0:T(1024)S(1)}, f32[1600]{0:T(1024)}, u32[]{:S(2)}) copy-start(f32[1600]{0:T(1024)} %param.16) | copy-start | bytes 19204
Sparse Core Ops, SparseCore 0:
  15.1 50.1 reduce-scatter.3
  130.1 256.6 all-reduce.3
  449.3 253.7 all-reduce.5
  708.5 38.9 all-gather.1
